TPU v7x, 32 devices: a whole 2x2x4 slice. The times are simulated.
32 devices in a mesh: case: 2 (over y), tm: 4 (over z), bundle: 2 (over x), sub: 2 (over core).
Axes of the slice: x: 2, y: 2, z: 4, core: 2. Of those that a mesh axis runs over, the one named last changes fastest.
Arguments:
- cotangent: bfloat16 [16384, 512], P(('case', 'tm'), 'bundle'), parts along dimension 0, may hold values from -28 to 28
- inputs: bfloat16 [16384, 512], P(('case', 'tm'), 'bundle'), parts along dimension 0, may hold values from -6 to 6
- impulse: bfloat16 [8, 128, 4096], P('bundle', 'sub'), may hold values from -0.0625 to 0.0625
- terminal: int32 [8, 64], P('bundle'), may hold values from 0 to 63, each once within a row
- fault_step: int32 [2], P('case'), parts along dimension 0, may hold values from 0 to 4095
Outputs:
- voltage_grad: bfloat16 [16384, 512], P(('case', 'tm', 'sub'), 'bundle'), parts along dimension 0
- impulse_grad: float32 [16, 128, 4096], P(('case', 'bundle'), 'sub', 'tm'), parts along dimension 0
There are 2 independent parts, one for each index of `case`. A program takes and returns all parts, laid end to end along the dimension named above; an argument that names none is the same for every part. Nothing has to cross between parts.
Inputs may be any that keep to these rules, and one draw needn't show every extreme that they name: Each row of terminal orders the 64 terminals of a bundle, each once.
All inputs are finite; a program needn't handle non-finite values.
Results may differ from a plain program's by a relative error of at most 0.001.
Values may be sent and summed in bfloat16 or wider, within the bound.
No kernel may reach another device: no remote copies, remote signals or barrier semaphores. Data moves between devices by JAX's collectives and lax.ppermute only.
A program may use at most 320 MiB of HBM per device.

v0:
```python
import math
import jax
import jax.numpy as jnp
from jax import lax
from jax.sharding import PartitionSpec as P

CB = 64
NB = 8
L = 128
norm_ratio = 0.5
tile_rows = 8


def passed_along(block, axis, distance):
    devices = range(lax.axis_size(axis))
    route = [(i - distance, i) for i in devices if i - distance in devices]
    return lax.ppermute(block, axis, route)


def tiles_of(source, start, block_rows, lag_count):
    bundles = source.shape[0]
    width = source.shape[2]
    window = lax.dynamic_slice_in_dim(source, start, block_rows + lag_count, 1)
    tiled = window.reshape(bundles, (block_rows + lag_count) // tile_rows, tile_rows, width)
    tile_count = block_rows // tile_rows
    spans = [tiled[:, first : first + tile_count] for first in range(lag_count // tile_rows + 1)]
    wide = jnp.concatenate(spans, axis=2)
    return wide.reshape(bundles, tile_count, (lag_count + tile_rows) * width)


def local(cotangent, inputs, impulse, terminal, fault_step):
    seg_rows = cotangent.shape[0]
    local_bundles = terminal.shape[0]
    bundle_width = terminal.shape[1]
    lag_count = impulse.shape[1]
    all_lags = lag_count * lax.axis_size("sub")
    lag_first = lax.axis_index("sub") * lag_count
    columns = jnp.arange(bundle_width, dtype=jnp.int32)
    onehot = (terminal[:, :, None] == columns[None, None, :]).astype(jnp.bfloat16)
    grad_in = cotangent.reshape(seg_rows, local_bundles, bundle_width)
    reordered = jnp.einsum(
        "tbi,bir->tbr", grad_in, onehot, preferred_element_type=jnp.float32
    ).astype(jnp.bfloat16)
    seg_start = lax.axis_index("tm") * seg_rows
    steps_here = seg_start + jnp.arange(seg_rows, dtype=jnp.int32)
    live_rows = steps_here >= fault_step[0]
    masked = jnp.where(
        live_rows[:, None, None],
        inputs.reshape(seg_rows, local_bundles, bundle_width),
        jnp.zeros((), jnp.bfloat16),
    )
    ahead_rows = passed_along(reordered[:all_lags], "tm", -1)
    extended = jnp.concatenate([reordered, ahead_rows], axis=0)
    ext_lanes = jnp.transpose(extended, (1, 0, 2))
    reord_lanes = jnp.transpose(reordered, (1, 0, 2))
    kernel = impulse.reshape(local_bundles, lag_count, bundle_width, bundle_width)
    zero_pad = jnp.zeros((local_bundles, tile_rows, bundle_width, bundle_width), jnp.bfloat16)
    kernel_pad = jnp.concatenate([zero_pad, kernel, zero_pad], axis=1)
    toeplitz = jnp.stack(
        [
            kernel_pad[:, tile_rows - shift_row : tile_rows - shift_row + lag_count + tile_rows]
            for shift_row in range(tile_rows)
        ],
        axis=3,
    )
    toeplitz = toeplitz.reshape(
        local_bundles, (lag_count + tile_rows) * bundle_width, tile_rows * bundle_width
    )
    block_rows = min(512, seg_rows)
    block_count = seg_rows // block_rows
    tile_count = block_rows // tile_rows
    behind = passed_along(masked[seg_rows - all_lags :], "tm", 1)
    history = jnp.concatenate([behind, masked], axis=0)
    hist_lanes = jnp.transpose(history, (1, 0, 2))

    def advance(grad_acc, block_index):
        row_start = block_index * block_rows
        wide = tiles_of(ext_lanes, row_start + lag_first, block_rows, lag_count)
        dx_block = jnp.einsum("bkx,bxy->bky", wide, toeplitz, preferred_element_type=jnp.float32)
        row_block = lax.dynamic_slice_in_dim(reord_lanes, row_start, block_rows, 1).reshape(
            local_bundles, tile_count, tile_rows * bundle_width
        )
        earlier = tiles_of(
            hist_lanes, row_start + all_lags - lag_first - lag_count, block_rows, lag_count
        )
        grad_acc = grad_acc + jnp.einsum(
            "bkx,bky->bxy", row_block, earlier, preferred_element_type=jnp.float32
        )
        return (grad_acc, dx_block.reshape(local_bundles, block_rows, bundle_width))

    acc_shape = (local_bundles, tile_rows * bundle_width, (lag_count + tile_rows) * bundle_width)
    grad_total, dx_blocks = lax.scan(
        advance, jnp.zeros(acc_shape, jnp.float32), jnp.arange(block_count, dtype=jnp.int32)
    )
    partial_dx = jnp.transpose(dx_blocks, (0, 2, 1, 3)).reshape(
        seg_rows, local_bundles * bundle_width
    )
    folded = grad_total.reshape(
        local_bundles, tile_rows, bundle_width, lag_count + tile_rows, bundle_width
    )
    lag_sum = folded[:, 0, :, 1 : lag_count + 1, :]
    for shift_row in range(1, tile_rows):
        lag_sum = lag_sum + folded[:, shift_row, :, shift_row + 1 : shift_row + lag_count + 1, :]
    grad_blocks = jnp.transpose(jnp.flip(lag_sum, axis=2), (0, 2, 1, 3))
    summed_dx = lax.psum_scatter(partial_dx, "sub", scatter_dimension=0, tiled=True)
    share_rows = summed_dx.shape[0]
    own_steps = (
        seg_start + lax.axis_index("sub") * share_rows + jnp.arange(share_rows, dtype=jnp.int32)
    )
    voltage_grad = jnp.where((own_steps >= fault_step[0])[:, None], summed_dx, 0.0).astype(
        jnp.bfloat16
    )
    grad_flat = grad_blocks.reshape(local_bundles, lag_count, bundle_width * bundle_width)
    grad_sum = lax.psum(grad_flat, "tm")
    share_cols = grad_flat.shape[2] // lax.axis_size("tm")
    own_grad = lax.dynamic_slice_in_dim(grad_sum, lax.axis_index("tm") * share_cols, share_cols, 2)
    own_squares = jnp.sum(own_grad * own_grad)
    total_squares = lax.psum(own_squares, ("tm", "bundle", "sub"))
    norm_limit = norm_ratio * math.sqrt(NB * L * CB * CB)
    factor = norm_limit / jnp.sqrt(total_squares + 1e-06)
    return (voltage_grad, own_grad * factor)


def solution(mesh):
    placed = (
        P(("case", "tm"), "bundle"),
        P(("case", "tm"), "bundle"),
        P("bundle", "sub", None),
        P("bundle", None),
        P("case"),
    )
    return jax.shard_map(
        local,
        mesh=mesh,
        in_specs=placed,
        out_specs=(P(("case", "tm", "sub"), "bundle"), P(("case", "bundle"), "sub", "tm")),
        check_vma=False,
    )
```

profile of v0, /device:TPU:0, one launch (start us, length us, event | category | flops | bytes accessed | tf_op | source)
XLA Modules:
  0.0 749.6 jit_solution(2607385197991196513)
XLA Ops:
  59.8 47.4 %copy.50 = bf16[4,72,64,8,64]{4,3,2,1,0:T(8,128)(2,1)} copy(bf16[4,72,64,8,64]{1,4,3,2,0:T(8,128)(2,1)} %fusion.1) | data formatting | bytes 37748736 | tf_op jit(solution)/shard_map/stack | solution.py:59
  107.2 49.1 %reshape.92 = bf16[4,4608,512]{2,1,0:T(8,128)(2,1)} reshape(bf16[4,72,64,8,64]{4,3,2,1,0:T(8,128)(2,1)} %copy.50) | data formatting | bytes 37748736 | tf_op jit(solution)/shard_map/reshape | solution.py:66
  159.7 269.9 %while.17 = (s32[]{:T(128)}, f32[4,512,4608]{2,1,0:T(8,128)}, f32[4,4,512,64]{3,2,1,0:T(8,128)}, s32[4]{0:T(128)S(1)}, bf16[4,2048,64]{1,2,0:T(8,128)(2,1)}, /*i...) while((s32[]{:T(128)}, f32[4,512,4608]{2,1,0:T(8,128)}, ...), condition=%wide.region_1.2_spmd.clone, body=%wide.region_0.1_spmd.clone.sunk | while | flops 2434793472 | bytes 131072384 | solution.py:92
  173.4 6.1 reshape.109
  179.5 8.1 %fusion.24 = f32[4,64,512]{2,1,0:T(8,128)S(1)} fusion(bf16[4,64,4608]{2,1,0:T(8,128)(2,1)S(1)} %reshape.109, bf16[4,4608,512]{2,1,0:T(8,128)(2,1)} %get-tuple-element.366), kind=kOutput, calls=%fused_computation.58.clone.1 | convolution fusion | flops 1207959552 | bytes 21757952 | tf_op jit(solution)/shard_map/while/body/eval_jaxpr/bkx,bxy->bky/dot_general | solution.py:79
  196.9 6.1 reshape.108
  203.1 14.0 %select_add_fusion.2 = f32[4,512,4608]{2,1,0:T(8,128)} fusion(f32[4,512,4608]{2,1,0:T(8,128)} %get-tuple-element.342, pred[]{:T(512)S(6)} %compare.4, bf16[4,64,512]{2,1,0:T(8,128)(2,1)S(1)} %copy-done.1, bf16[4,64,4608]{2,1,0:T(8,128)(2,1)S(1)} %reshape.108), kind=kOutput, calls=%fused_computation.clone.1 | convolution fusion | flops 1226833920 | bytes 78118912 | tf_op jit(solution)/shard_map/while/body/eval_jaxpr/bkx,bky->bxy/dot_general | solution.py:86
  230.8 6.1 reshape.109
  236.9 8.1 %fusion.24 = f32[4,64,512]{2,1,0:T(8,128)S(1)} fusion(bf16[4,64,4608]{2,1,0:T(8,128)(2,1)S(1)} %reshape.109, bf16[4,4608,512]{2,1,0:T(8,128)(2,1)} %get-tuple-element.366), kind=kOutput, calls=%fused_computation.58.clone.1 | convolution fusion | flops 1207959552 | bytes 21757952 | tf_op jit(solution)/shard_map/while/body/eval_jaxpr/bkx,bxy->bky/dot_general | solution.py:79
  254.4 6.1 reshape.108
  260.5 27.4 %select_add_fusion.2 = f32[4,512,4608]{2,1,0:T(8,128)} fusion(f32[4,512,4608]{2,1,0:T(8,128)} %get-tuple-element.342, pred[]{:T(512)S(6)} %compare.4, bf16[4,64,512]{2,1,0:T(8,128)(2,1)S(1)} %copy-done.1, bf16[4,64,4608]{2,1,0:T(8,128)(2,1)S(1)} %reshape.108), kind=kOutput, calls=%fused_computation.clone.1 | convolution fusion | flops 1226833920 | bytes 78118912 | tf_op jit(solution)/shard_map/while/body/eval_jaxpr/bkx,bky->bxy/dot_general | solution.py:86
  301.6 6.1 reshape.109
  307.8 8.1 %fusion.24 = f32[4,64,512]{2,1,0:T(8,128)S(1)} fusion(bf16[4,64,4608]{2,1,0:T(8,128)(2,1)S(1)} %reshape.109, bf16[4,4608,512]{2,1,0:T(8,128)(2,1)} %get-tuple-element.366), kind=kOutput, calls=%fused_computation.58.clone.1 | convolution fusion | flops 1207959552 | bytes 21757952 | tf_op jit(solution)/shard_map/while/body/eval_jaxpr/bkx,bxy->bky/dot_general | solution.py:79
  331.4 27.4 %select_add_fusion.2 = f32[4,512,4608]{2,1,0:T(8,128)} fusion(f32[4,512,4608]{2,1,0:T(8,128)} %get-tuple-element.342, pred[]{:T(512)S(6)} %compare.4, bf16[4,64,512]{2,1,0:T(8,128)(2,1)S(1)} %copy-done.1, bf16[4,64,4608]{2,1,0:T(8,128)(2,1)S(1)} %reshape.108), kind=kOutput, calls=%fused_computation.clone.1 | convolution fusion | flops 1226833920 | bytes 78118912 | tf_op jit(solution)/shard_map/while/body/eval_jaxpr/bkx,bky->bxy/dot_general | solution.py:86
  378.6 8.1 %fusion.24 = f32[4,64,512]{2,1,0:T(8,128)S(1)} fusion(bf16[4,64,4608]{2,1,0:T(8,128)(2,1)S(1)} %reshape.109, bf16[4,4608,512]{2,1,0:T(8,128)(2,1)} %get-tuple-element.366), kind=kOutput, calls=%fused_computation.58.clone.1 | convolution fusion | flops 1207959552 | bytes 21757952 | tf_op jit(solution)/shard_map/while/body/eval_jaxpr/bkx,bxy->bky/dot_general | solution.py:79
  396.0 6.1 reshape.108
  402.2 27.4 %select_add_fusion.2 = f32[4,512,4608]{2,1,0:T(8,128)} fusion(f32[4,512,4608]{2,1,0:T(8,128)} %get-tuple-element.342, pred[]{:T(512)S(6)} %compare.4, bf16[4,64,512]{2,1,0:T(8,128)(2,1)S(1)} %copy-done.1, bf16[4,64,4608]{2,1,0:T(8,128)(2,1)S(1)} %reshape.108), kind=kOutput, calls=%fused_computation.clone.1 | convolution fusion | flops 1226833920 | bytes 78118912 | tf_op jit(solution)/shard_map/while/body/eval_jaxpr/bkx,bky->bxy/dot_general | solution.py:86
  435.6 54.3 %reshape.94 = f32[4,8,64,72,64]{4,3,2,1,0:T(8,128)} reshape(f32[4,512,4608]{2,1,0:T(8,128)} %get-tuple-element.183) | data formatting | bytes 75497472 | tf_op jit(solution)/shard_map/reshape | solution.py:98
  489.9 27.4 %fusion = f32[4,64,64,64]{3,2,1,0:T(8,128)} fusion(f32[4,8,64,72,64]{4,3,2,1,0:T(8,128)} %reshape.94), kind=kLoop, calls=%fused_computation.24 | loop fusion | flops 7340032 | bytes 37748736 | tf_op jit(solution)/shard_map/add | solution.py:103
  517.3 11.9 %rev.4 = f32[4,64,64,64]{3,2,1,0:T(8,128)} reverse(f32[4,64,64,64]{3,2,1,0:T(8,128)} %fusion), dimensions={2} | reverse | bytes 8388608 | tf_op jit(solution)/shard_map/jit(_flip)/rev | solution.py:104
  529.1 11.5 %copy.55 = f32[4,64,64,64]{3,2,1,0:T(8,128)} copy(f32[4,64,64,64]{3,1,2,0:T(8,128)} %bitcast.113) | data formatting | bytes 8388608 | tf_op jit(solution)/shard_map/transpose | solution.py:104
  540.6 7.9 %reshape.95 = f32[4,64,4096]{2,1,0:T(8,128)} reshape(f32[4,64,64,64]{3,2,1,0:T(8,128)} %copy.55) | data formatting | bytes 8388608 | tf_op jit(solution)/shard_map/reshape | solution.py:113
  549.9 154.3 %all-reduce.3.cloned.1.call-done = f32[4,64,4096]{2,1,0:T(8,128)} async-done(((f32[4,64,4096]{2,1,0:T(8,128)}), f32[4,64,4096]{2,1,0:T(8,128)}) %all-reduce.3.cloned.1.call-update) | async-done | bytes 4194320 | tf_op jit(solution)/shard_map/psum | solution.py:114
  707.3 31.9 %psum.15 = f32[]{:T(128)} all-reduce(f32[]{:T(128)} %multiply_reduce_fusion), channel_id=1, replica_groups=mesh['case'=2,'tm'=4,'bundle'=2,'sub'=2] {'tm','bundle','sub'}, use_global_device_ids=true, to_apply=%region_5.6 | all-reduce | flops 1 | bytes 8 | tf_op jit(solution)/shard_map/psum | solution.py:118
  (161 shorter events, 168.4 us)
Async XLA Ops:
  8.0 6.5 copy-start.2
  8.0 540.5 %reduce-scatter.2.cloned.1.call-start = ((), (), s32[]{:S(2)}) async-start(), calls=%async_computation.1 | async-start | bytes 3145728 | tf_op jit(solution)/shard_map/reduce_scatter | solution.py:105
  12.5 143.7 %collective-permute-start.1 = (bf16[128,4,64]{0,2,1:T(8,128)(2,1)S(1)}, bf16[128,4,64]{0,2,1:T(8,128)(2,1)S(1)}, u32[]{:S(2)}, u32[]{:S(2)}) collective-permute-start(bf16[128,4,64]{0,2,1:T(8,128)(2,1)S(1)} %slice.269), channel_id=1, source_target_pairs={{4,0},{8,4},{12,8},{5,1},{9,5},{13,9},{6,2},{10,6},{14,10},{7,3},{... | collective-permute-start | bytes 196616 | tf_op jit(solution)/shard_map/ppermute | solution.py:17
  15.3 143.3 %collective-permute-start = (bf16[128,4,64]{0,2,1:T(8,128)(2,1)S(1)}, bf16[128,4,64]{0,2,1:T(8,128)(2,1)S(1)}, u32[]{:S(2)}, u32[]{:S(2)}) collective-permute-start(bf16[128,4,64]{0,2,1:T(8,128)(2,1)S(1)} %slice.268), channel_id=1, source_target_pairs={{0,4},{4,8},{8,12},{1,5},{5,9},{9,13},{2,6},{6,10},{10,14},{3,7},{... | collective-permute-start | bytes 196616 | tf_op jit(solution)/shard_map/ppermute | solution.py:17
  25.6 7.2 copy-start
  195.2 7.9 %copy-start.1 = (bf16[4,64,512]{2,1,0:T(8,128)(2,1)S(1)}, bf16[4,64,512]{2,1,0:T(8,128)(2,1)}, u32[]{:S(2)}) copy-start(bf16[4,64,512]{2,1,0:T(8,128)(2,1)} %reshape.107) | copy-start | bytes 786436 | tf_op jit(solution)/shard_map/while
  252.6 7.9 %copy-start.1 = (bf16[4,64,512]{2,1,0:T(8,128)(2,1)S(1)}, bf16[4,64,512]{2,1,0:T(8,128)(2,1)}, u32[]{:S(2)}) copy-start(bf16[4,64,512]{2,1,0:T(8,128)(2,1)} %reshape.107) | copy-start | bytes 786436 | tf_op jit(solution)/shard_map/while
  323.4 7.9 %copy-start.1 = (bf16[4,64,512]{2,1,0:T(8,128)(2,1)S(1)}, bf16[4,64,512]{2,1,0:T(8,128)(2,1)}, u32[]{:S(2)}) copy-start(bf16[4,64,512]{2,1,0:T(8,128)(2,1)} %reshape.107) | copy-start | bytes 786436 | tf_op jit(solution)/shard_map/while
  394.2 7.9 %copy-start.1 = (bf16[4,64,512]{2,1,0:T(8,128)(2,1)S(1)}, bf16[4,64,512]{2,1,0:T(8,128)(2,1)}, u32[]{:S(2)}) copy-start(bf16[4,64,512]{2,1,0:T(8,128)(2,1)} %reshape.107) | copy-start | bytes 786436 | tf_op jit(solution)/shard_map/while
  435.5 268.7 %all-reduce.3.cloned.1.call-start = ((), (), s32[]{:S(2)}) async-start(), calls=%async_computation.2 | async-start | bytes 8388608 | tf_op jit(solution)/shard_map/psum | solution.py:114
Sparse Core Ops, SparseCore 0:
  435.7 10.2 reduce-scatter.1
Sparse Core Ops, SparseCore 1:
  548.6 155.6 all-reduce.2
where the time goes:
time: 755 us; the launch traced here: 750 us
  local copies, waits for them, and re-layouts  365 us (48%)
  waiting for transfers between devices  154 us (20%)
  matrix products  131 us (17%)
  other arithmetic  40.7 us (5%)
  blocking collectives  31.9 us (4%)
  between operations  17 us (2%)
    psum x1, waiting for transfers between devices, local(): grad_sum = lax.psum(grad_flat, 'tm')  154 us
    dot_general x4, matrix products, advance(): jnp.einsum('bkx,bky->bxy', row_block, earlier, preferred_element_type=jnp...  96.3 us
    while x72, local copies, waits for them, and re-layouts  56.9 us
    reshape x1, local copies, waits for them, and re-layouts, local(): grad_total.reshape(local_bundles, tile_rows, bundle_width, lag_count + ti...  54.3 us
    another operation x2, local copies, waits for them, and re-layouts, local(): jnp.stack([kernel_pad[:, tile_rows - shift_row:tile_rows - shift_row + la...  50.8 us
    reshape x8, local copies, waits for them, and re-layouts, tiles_of(): return wide.reshape(bundles, tile_count, (lag_count + tile_rows) * width)  49.2 us
    reshape x1, local copies, waits for them, and re-layouts, local(): toeplitz.reshape(local_bundles, (lag_count + tile_rows) * bundle_width, t...  49.1 us
    unnamed x16, local copies, waits for them, and re-layouts  35.8 us
  transfers between devices with their start and end apart: 4, of which 1 were waited for; matrix products, arithmetic and copies ran while one was open for 34% of the time, Pallas kernels for 0%

commit v1 on v0

--- a/solution.py
+++ b/solution.py
@@ -111,7 +111,9 @@
         jnp.bfloat16
     )
     grad_flat = grad_blocks.reshape(local_bundles, lag_count, bundle_width * bundle_width)
-    grad_sum = lax.psum(grad_flat, "tm")
+    grad_sum = grad_flat
+    for hop in (1, 2):
+        grad_sum = grad_sum + lax.ppermute(grad_sum, "tm", [(dev, dev ^ hop) for dev in range(4)])
     share_cols = grad_flat.shape[2] // lax.axis_size("tm")
     own_grad = lax.dynamic_slice_in_dim(grad_sum, lax.axis_index("tm") * share_cols, share_cols, 2)
     own_squares = jnp.sum(own_grad * own_grad)

time: 755 us -> 874 us (1.16)
  waiting for transfers between devices: 154 us -> 263 us
    ppermute x0 -> x2, waiting for transfers between devices: none -> 263 us  [local(): lax.ppermute(grad_sum, 'tm', [(dev, dev ^ hop) for dev in range(4)])]
    psum x1 -> x0, waiting for transfers between devices: 154 us -> none  [local(): grad_sum = lax.psum(grad_flat, 'tm')]
  transfers between devices with their start and end apart: 4 -> 5, of which waited for: 1 -> 2; matrix products, arithmetic and copies ran while one was open for 34% -> 17% of each run, Pallas kernels for 0% -> 0%
where the time goes in v1:
time: 874 us; the launch traced here: 868 us
  local copies, waits for them, and re-layouts  365 us (42%)
  waiting for transfers between devices  263 us (30%)
  matrix products  131 us (15%)
  other arithmetic  47.5 us (5%)
  blocking collectives  32.2 us (4%)
  between operations  15.5 us (2%)
  starting transfers between devices  11.7 us (1%)
    ppermute x2, waiting for transfers between devices, local(): lax.ppermute(grad_sum, 'tm', [(dev, dev ^ hop) for dev in range(4)])  263 us
    dot_general x4, matrix products, advance(): jnp.einsum('bkx,bky->bxy', row_block, earlier, preferred_element_type=jnp...  96.4 us
    while x72, local copies, waits for them, and re-layouts  56.2 us
    reshape x1, local copies, waits for them, and re-layouts, local(): grad_total.reshape(local_bundles, tile_rows, bundle_width, lag_count + ti...  54 us
    another operation x2, local copies, waits for them, and re-layouts, local(): jnp.stack([kernel_pad[:, tile_rows - shift_row:tile_rows - shift_row + la...  50.7 us
    reshape x8, local copies, waits for them, and re-layouts, tiles_of(): return wide.reshape(bundles, tile_count, (lag_count + tile_rows) * width)  49.2 us
    reshape x1, local copies, waits for them, and re-layouts, local(): toeplitz.reshape(local_bundles, (lag_count + tile_rows) * bundle_width, t...  49.1 us
    unnamed x16, local copies, waits for them, and re-layouts  36 us
  transfers between devices with their start and end apart: 5, of which 2 were waited for; matrix products, arithmetic and copies ran while one was open for 17% of the time, Pallas kernels for 0%

profile of v1, /device:TPU:0, one launch (start us, length us, event | category | flops | bytes accessed | tf_op | source)
XLA Modules:
  0.0 868.1 jit_solution(16481597088719214614)
XLA Ops:
  58.9 47.4 %copy.50 = bf16[4,72,64,8,64]{4,3,2,1,0:T(8,128)(2,1)} copy(bf16[4,72,64,8,64]{1,4,3,2,0:T(8,128)(2,1)} %fusion.1) | data formatting | bytes 37748736 | tf_op jit(solution)/shard_map/stack | solution.py:59
  106.4 49.1 %reshape.92 = bf16[4,4608,512]{2,1,0:T(8,128)(2,1)} reshape(bf16[4,72,64,8,64]{4,3,2,1,0:T(8,128)(2,1)} %copy.50) | data formatting | bytes 37748736 | tf_op jit(solution)/shard_map/reshape | solution.py:66
  158.9 269.9 %while.17 = (s32[]{:T(128)}, f32[4,512,4608]{2,1,0:T(8,128)}, f32[4,4,512,64]{3,2,1,0:T(8,128)}, s32[4]{0:T(128)S(1)}, bf16[4,2048,64]{1,2,0:T(8,128)(2,1)}, /*i...) while((s32[]{:T(128)}, f32[4,512,4608]{2,1,0:T(8,128)}, ...), condition=%wide.region_1.2_spmd.clone, body=%wide.region_0.1_spmd.clone.sunk | while | flops 2434793472 | bytes 131072384 | solution.py:92
  172.6 6.1 reshape.109
  178.7 8.1 fusion.24
  196.1 6.1 reshape.108
  202.3 14.0 %select_add_fusion.2 = f32[4,512,4608]{2,1,0:T(8,128)} fusion(f32[4,512,4608]{2,1,0:T(8,128)} %get-tuple-element.342, pred[]{:T(512)S(6)} %compare.4, bf16[4,64,512]{2,1,0:T(8,128)(2,1)S(1)} %copy-done.1, bf16[4,64,4608]{2,1,0:T(8,128)(2,1)S(1)} %reshape.108), kind=kOutput, calls=%fused_computation.clone.1 | convolution fusion | flops 1226833920 | bytes 78118912 | tf_op jit(solution)/shard_map/while/body/eval_jaxpr/bkx,bky->bxy/dot_general | solution.py:86
  229.9 6.1 reshape.109
  236.0 8.1 fusion.24
  253.5 6.1 reshape.108
  259.6 27.5 %select_add_fusion.2 = f32[4,512,4608]{2,1,0:T(8,128)} fusion(f32[4,512,4608]{2,1,0:T(8,128)} %get-tuple-element.342, pred[]{:T(512)S(6)} %compare.4, bf16[4,64,512]{2,1,0:T(8,128)(2,1)S(1)} %copy-done.1, bf16[4,64,4608]{2,1,0:T(8,128)(2,1)S(1)} %reshape.108), kind=kOutput, calls=%fused_computation.clone.1 | convolution fusion | flops 1226833920 | bytes 78118912 | tf_op jit(solution)/shard_map/while/body/eval_jaxpr/bkx,bky->bxy/dot_general | solution.py:86
  300.8 6.1 reshape.109
  306.9 8.1 fusion.24
  330.5 27.5 %select_add_fusion.2 = f32[4,512,4608]{2,1,0:T(8,128)} fusion(f32[4,512,4608]{2,1,0:T(8,128)} %get-tuple-element.342, pred[]{:T(512)S(6)} %compare.4, bf16[4,64,512]{2,1,0:T(8,128)(2,1)S(1)} %copy-done.1, bf16[4,64,4608]{2,1,0:T(8,128)(2,1)S(1)} %reshape.108), kind=kOutput, calls=%fused_computation.clone.1 | convolution fusion | flops 1226833920 | bytes 78118912 | tf_op jit(solution)/shard_map/while/body/eval_jaxpr/bkx,bky->bxy/dot_general | solution.py:86
  377.7 8.1 fusion.24
  401.3 27.5 %select_add_fusion.2 = f32[4,512,4608]{2,1,0:T(8,128)} fusion(f32[4,512,4608]{2,1,0:T(8,128)} %get-tuple-element.342, pred[]{:T(512)S(6)} %compare.4, bf16[4,64,512]{2,1,0:T(8,128)(2,1)S(1)} %copy-done.1, bf16[4,64,4608]{2,1,0:T(8,128)(2,1)S(1)} %reshape.108), kind=kOutput, calls=%fused_computation.clone.1 | convolution fusion | flops 1226833920 | bytes 78118912 | tf_op jit(solution)/shard_map/while/body/eval_jaxpr/bkx,bky->bxy/dot_general | solution.py:86
  428.8 54.0 %reshape.94 = f32[4,8,64,72,64]{4,3,2,1,0:T(8,128)} reshape(f32[4,512,4608]{2,1,0:T(8,128)} %get-tuple-element.183) | data formatting | bytes 75497472 | tf_op jit(solution)/shard_map/reshape | solution.py:98
  482.8 27.4 %fusion = f32[4,64,64,64]{3,2,1,0:T(8,128)} fusion(f32[4,8,64,72,64]{4,3,2,1,0:T(8,128)} %reshape.94), kind=kLoop, calls=%fused_computation.24 | loop fusion | flops 7340032 | bytes 37748736 | tf_op jit(solution)/shard_map/add | solution.py:103
  510.2 11.9 %rev.4 = f32[4,64,64,64]{3,2,1,0:T(8,128)} reverse(f32[4,64,64,64]{3,2,1,0:T(8,128)} %fusion), dimensions={2} | reverse | bytes 8388608 | tf_op jit(solution)/shard_map/jit(_flip)/rev | solution.py:104
  522.1 11.5 %copy.55 = f32[4,64,64,64]{3,2,1,0:T(8,128)} copy(f32[4,64,64,64]{3,1,2,0:T(8,128)} %bitcast.113) | data formatting | bytes 8388608 | tf_op jit(solution)/shard_map/transpose | solution.py:104
  533.6 7.9 reshape.95
  549.5 84.4 %collective-permute-done.2 = f32[4,64,4096]{2,1,0:T(8,128)} collective-permute-done((f32[4,64,4096]{2,1,0:T(8,128)}, f32[4,64,4096]{2,1,0:T(8,128)}, u32[]{:S(2)}, u32[]{:S(2)}) %collective-permute-start.2) | collective-permute-done | bytes 4194336 | tf_op jit(solution)/shard_map/ppermute | solution.py:116
  644.0 178.2 %collective-permute-done.3 = f32[4,64,4096]{2,1,0:T(8,128)} collective-permute-done((f32[4,64,4096]{2,1,0:T(8,128)}, f32[4,64,4096]{2,1,0:T(8,128)}, u32[]{:S(2)}, u32[]{:S(2)}) %collective-permute-start.3) | collective-permute-done | bytes 4194336 | tf_op jit(solution)/shard_map/ppermute | solution.py:116
  825.6 32.2 %psum.7 = f32[]{:T(128)} all-reduce(f32[]{:T(128)} %multiply_reduce_fusion), channel_id=1, replica_groups=mesh['case'=2,'tm'=4,'bundle'=2,'sub'=2] {'tm','bundle','sub'}, use_global_device_ids=true, to_apply=%region_4.5 | all-reduce | flops 1 | bytes 8 | tf_op jit(solution)/shard_map/psum | solution.py:120
  (163 shorter events, 185.9 us)
Async XLA Ops:
  7.2 6.5 copy-start.2
  7.2 635.5 %reduce-scatter.2.cloned.1.call-start = ((), (), s32[]{:S(2)}) async-start(), calls=%async_computation.1 | async-start | bytes 3145728 | tf_op jit(solution)/shard_map/reduce_scatter | solution.py:105
  11.7 143.8 %collective-permute-start.1 = (bf16[128,4,64]{0,2,1:T(8,128)(2,1)S(1)}, bf16[128,4,64]{0,2,1:T(8,128)(2,1)S(1)}, u32[]{:S(2)}, u32[]{:S(2)}) collective-permute-start(bf16[128,4,64]{0,2,1:T(8,128)(2,1)S(1)} %slice.269), channel_id=1, source_target_pairs={{4,0},{8,4},{12,8},{5,1},{9,5},{13,9},{6,2},{10,6},{14,10},{7,3},{... | collective-permute-start | bytes 196616 | tf_op jit(solution)/shard_map/ppermute | solution.py:17
  14.4 143.4 %collective-permute-start = (bf16[128,4,64]{0,2,1:T(8,128)(2,1)S(1)}, bf16[128,4,64]{0,2,1:T(8,128)(2,1)S(1)}, u32[]{:S(2)}, u32[]{:S(2)}) collective-permute-start(bf16[128,4,64]{0,2,1:T(8,128)(2,1)S(1)} %slice.268), channel_id=1, source_target_pairs={{0,4},{4,8},{8,12},{1,5},{5,9},{9,13},{2,6},{6,10},{10,14},{3,7},{... | collective-permute-start | bytes 196616 | tf_op jit(solution)/shard_map/ppermute | solution.py:17
  24.8 7.2 copy-start
  194.2 8.0 copy-start.1
  251.6 8.0 copy-start.1
  322.5 8.0 copy-start.1
  393.3 8.0 copy-start.1
  541.5 92.3 %collective-permute-start.2 = (f32[4,64,4096]{2,1,0:T(8,128)}, f32[4,64,4096]{2,1,0:T(8,128)}, u32[]{:S(2)}, u32[]{:S(2)}) collective-permute-start(f32[4,64,4096]{2,1,0:T(8,128)} %reshape.95), channel_id=1, source_target_pairs={{0,4},{4,0},{8,12},{12,8},{1,5},{5,1},{9,13},{13,9},{2,6},{6,2},{1... | collective-permute-start | bytes 12582920 | tf_op jit(solution)/shard_map/ppermute | solution.py:116
  639.9 182.3 %collective-permute-start.3 = (f32[4,64,4096]{2,1,0:T(8,128)}, f32[4,64,4096]{2,1,0:T(8,128)}, u32[]{:S(2)}, u32[]{:S(2)}) collective-permute-start(f32[4,64,4096]{2,1,0:T(8,128)} %add.155), channel_id=1, source_target_pairs={{0,8},{4,12},{8,0},{12,4},{1,9},{5,13},{9,1},{13,5},{2,10},{6,14},... | collective-permute-start | bytes 12582920 | tf_op jit(solution)/shard_map/ppermute | solution.py:116
Sparse Core Ops, SparseCore 0:
  549.6 9.7 reduce-scatter.1
